TPU v7x, 256 devices: a whole 4x4x8 slice. The times are simulated.
256 devices in a mesh: dp: 8 (over y, x_hi), shard: 32 (over x_lo, z, core).
Axes of the slice: x: 4 (x_hi: 2, x_lo: 2; x = x_hi * 2 + x_lo), y: 4, z: 8, core: 2. Of those that a mesh axis runs over, the one named last changes fastest.
Arguments:
- grads: float32 [8, 1, 2, 4096, 4096], P('dp', None, None, None, 'shard'), may hold values from -6 to 6
- params: float32 [1, 2, 4096, 4096], P(None, None, ('dp', 'shard')), may hold values from -0.09375 to 0.09375
- moment_one: float32 [1, 2, 4096, 4096], P(None, None, ('dp', 'shard')), may hold values from -0.75 to 0.75
- moment_two: float32 [1, 2, 4096, 4096], P(None, None, ('dp', 'shard')), may hold values from 1e-05 to 0.01
- relation_ids: int32 [1], replicated, may hold values from 0 to 63
- rates: float32 [64], replicated, may hold values from 0.02 to 0.1
- step_count: int32 [1], replicated, may hold values from 1 to 8
Outputs:
- new_params: float32 [1, 2, 4096, 4096], P(None, None, ('dp', 'shard'))
- new_moment_one: float32 [1, 2, 4096, 4096], P(None, None, ('dp', 'shard'))
- new_moment_two: float32 [1, 2, 4096, 4096], P(None, None, ('dp', 'shard'))
- panels: bfloat16 [1, 2, 4096, 4096], P(None, None, None, 'shard')
Inputs may be any that keep to these rules, and one draw needn't show every extreme that they name: `relation_ids`: relation ids are edge types. `step_count`: the step count is positive.
All inputs are finite; a program needn't handle non-finite values.
Results may differ from a plain program's by a relative error of at most 0.001.
Values may be sent and summed in bfloat16 or wider, within the bound.
No kernel may reach another device: no remote copies, remote signals or barrier semaphores. Data moves between devices by JAX's collectives and lax.ppermute only.
A program may use at most 128 MiB of HBM per device.

v0:
```python
import jax
import jax.numpy as jnp
from jax import lax
from jax.sharding import PartitionSpec as P


def body(grads, params, moment_one, moment_two, relation_ids, rates, step_count):
    groups = lax.axis_size("dp")
    owners = lax.axis_size("shard")
    relations = grads.shape[1]
    panel_cols = grads.shape[-1]
    width = panel_cols * owners
    owned = params.shape[2]
    pieces = grads.reshape(relations, 2, groups, owners, owned, panel_cols)
    moved = lax.all_to_all(pieces, "shard", split_axis=3, concat_axis=5, tiled=True)
    summed = lax.psum_scatter(moved, "dp", scatter_dimension=2, tiled=True)
    gradient = summed.reshape(relations, 2, owned, width) / groups
    onehot = (relation_ids[:, None] == jnp.arange(rates.shape[0], dtype=jnp.int32)[None, :]).astype(
        jnp.float32
    )
    learn = jnp.sum(onehot * rates[None, :], axis=1)[:, None, None, None]
    new_one = 0.9 * moment_one + 0.1 * gradient
    new_two = 0.95 * moment_two + 0.05 * gradient * gradient
    steps = step_count[0].astype(jnp.float32)
    fix_one = 1.0 - jnp.power(jnp.float32(0.9), steps)
    fix_two = 1.0 - jnp.power(jnp.float32(0.95), steps)
    update = new_one / fix_one / (jnp.sqrt(new_two / fix_two) + 1e-08) + 0.1 * params
    new_params = params - learn * update
    fresh = new_params.astype(jnp.bfloat16).reshape(relations, 2, 1, 1, owned, width)
    stacked = lax.all_gather(fresh, "dp", axis=2, tiled=True)
    panel = lax.all_to_all(stacked, "shard", split_axis=5, concat_axis=3, tiled=True)
    panels = panel.reshape(relations, 2, width, panel_cols)
    return (new_params, new_one, new_two, panels)


def solution(mesh):
    in_specs = (
        P("dp", None, None, None, "shard"),
        P(None, None, ("dp", "shard"), None),
        P(None, None, ("dp", "shard"), None),
        P(None, None, ("dp", "shard"), None),
        P(),
        P(),
        P(),
    )
    out_specs = (
        P(None, None, ("dp", "shard"), None),
        P(None, None, ("dp", "shard"), None),
        P(None, None, ("dp", "shard"), None),
        P(None, None, None, "shard"),
    )
    return jax.shard_map(body, mesh=mesh, in_specs=in_specs, out_specs=out_specs, check_vma=False)
```

profile of v0, /device:TPU:32, one launch (start us, length us, event | category | flops | bytes accessed | tf_op | source)
XLA Modules:
  0.0 405.4 jit_solution(11220922597998962744)
XLA Ops:
  7.2 0.0 reduce-scatter.2.cloned.1.call-start
  7.2 2.8 copy.31
  10.1 105.8 %all_to_all.33 = f32[1,2,8,32,16,128]{5,4,1,2,0,3:T(8,128)S(1)} all-to-all(f32[1,2,8,32,16,128]{5,4,1,2,0,3:T(8,128)S(1)} %copy.31), channel_id=1, replica_groups=mesh['dp'=8,'shard'=32] {'shard'}, dimensions={3} | all-to-all | bytes 8388608 | tf_op jit(solution)/shard_map/all_to_all | solution.py:15
  115.9 2.4 copy.32
  118.3 5.7 %copy.33 = f32[1,2,8,1,16,4096]{5,4,3,1,0,2:T(8,128)} copy(f32[1,2,8,1,16,4096]{5,3,4,2,1,0:T(1,128)S(1)} %bitcast.38) | data formatting | bytes 8388608 | tf_op jit(solution)/shard_map/all_to_all | solution.py:15
  124.0 0.0 copy-start.3
  124.0 0.0 copy-start
  124.0 0.0 copy-start.1
  124.0 0.0 copy-start.2
  124.1 0.0 reduce-scatter.2.cloned.1.call-update
  124.1 0.0 all-gather.3.cloned.1.call-start
  125.6 0.0 copy-done.3
  125.6 0.7 fusion.1
  126.3 85.0 %reduce-scatter.2.cloned.1.call-done = f32[1,2,1,1,16,4096]{5,4,3,1,0,2:T(8,128)} async-done(((f32[1,2,8,1,16,4096]{5,4,3,1,0,2:T(8,128)}), f32[1,2,1,1,16,4096]{5,4,3,1,0,2:T(8,128)}) %reduce-scatter.2.cloned.1.call-update) | async-done | bytes 524304 | tf_op jit(solution)/shard_map/reduce_scatter | solution.py:16
  211.3 0.0 copy-done
  211.3 0.0 copy-done.1
  211.3 0.0 copy-done.2
  211.3 3.2 fusion.2
  214.5 0.0 all-gather.3.cloned.1.call-update
  214.6 57.6 %all-gather.3.cloned.1.call-done = bf16[1,2,128,4096]{3,2,1,0:T(8,128)(2,1)} async-done(((bf16[1,2,16,4096]{3,2,1,0:T(8,128)(2,1)}), bf16[1,2,128,4096]{3,2,1,0:T(8,128)(2,1)}) %all-gather.3.cloned.1.call-update) | async-done | bytes 2097168 | tf_op jit(solution)/shard_map/all_gather | solution.py:30
  272.1 15.3 %copy.37 = bf16[1,2,8,1,16,4096]{4,2,1,3,0,5:T(8,128)(2,1)} copy(bf16[1,2,8,1,16,4096]{5,4,2,1,3,0:T(8,128)(2,1)} %bitcast.41) | data formatting | bytes 4194304 | tf_op jit(solution)/shard_map/all_gather | solution.py:30
  287.4 19.7 %reshape.90 = bf16[32,2,16384]{2,1,0:T(2,128)(2,1)S(1)} reshape(bf16[4096,1,1,2,8,16]{5,4,3,2,1,0:T(8,128)(2,1)} %bitcast.36) | data formatting | bytes 4194304
  307.2 59.0 %all_to_all.34 = bf16[32,2,16384]{2,1,0:T(2,128)(2,1)} all-to-all(bf16[32,2,16384]{2,1,0:T(2,128)(2,1)S(1)} %reshape.90), channel_id=1, replica_groups=mesh['dp'=8,'shard'=32] {'shard'}, dimensions={0} | all-to-all | bytes 4194304 | tf_op jit(solution)/shard_map/all_to_all | solution.py:31
  366.2 16.4 %reshape.91 = bf16[4096,1,1,2,8,16]{5,4,3,2,1,0:T(8,128)(2,1)} reshape(bf16[32,2,16384]{2,1,0:T(2,128)(2,1)} %all_to_all.34) | data formatting | bytes 4194304
  382.6 13.7 %copy.40 = bf16[1,2,8,1,16,32,128]{6,5,4,2,1,3,0:T(8,128)(2,1)S(1)} copy(bf16[1,2,8,1,16,32,128]{4,2,1,6,5,3,0:T(8,128)(2,1)} %bitcast.37) | data formatting | bytes 4194304 | tf_op jit(solution)/shard_map/all_to_all | solution.py:31
  396.4 2.2 copy.39
Async XLA Ops:
  7.2 204.2 %reduce-scatter.2.cloned.1.call-start = ((), (), s32[]{:S(2)}) async-start(), calls=%async_computation.3 | async-start | bytes 4718592 | tf_op jit(solution)/shard_map/reduce_scatter | solution.py:16
  124.0 1.6 copy-start.3
  124.0 87.3 %copy-start = (f32[1,2,16,4096]{3,2,1,0:T(8,128)S(1)}, f32[1,2,16,4096]{3,2,1,0:T(8,128)}, u32[]{:S(2)}) copy-start(f32[1,2,16,4096]{3,2,1,0:T(8,128)} %param.8) | copy-start | bytes 1572868
  124.0 87.3 %copy-start.1 = (f32[1,2,16,4096]{3,2,1,0:T(8,128)S(1)}, f32[1,2,16,4096]{3,2,1,0:T(8,128)}, u32[]{:S(2)}) copy-start(f32[1,2,16,4096]{3,2,1,0:T(8,128)} %param.10) | copy-start | bytes 1572868
  124.0 87.3 %copy-start.2 = (f32[1,2,16,4096]{3,2,1,0:T(8,128)S(1)}, f32[1,2,16,4096]{3,2,1,0:T(8,128)}, u32[]{:S(2)}) copy-start(f32[1,2,16,4096]{3,2,1,0:T(8,128)} %param.9) | copy-start | bytes 1572868
  124.1 148.1 %all-gather.3.cloned.1.call-start = ((), (), s32[]{:S(2)}) async-start(), calls=%async_computation.4 | async-start | bytes 2359296 | tf_op jit(solution)/shard_map/all_gather | solution.py:30
Sparse Core Ops, SparseCore 0:
  124.2 87.0 reduce-scatter.1
  214.7 57.4 all-gather.2
where the time goes:
time: 407 us; the launch traced here: 405 us
  blocking collectives  165 us (41%)
  waiting for transfers between devices  143 us (35%)
  local copies, waits for them, and re-layouts  78.4 us (19%)
  between operations  15.6 us (4%)
    all_to_all x1, blocking collectives, body(): lax.all_to_all(pieces, 'shard', split_axis=3, concat_axis=5, tiled=True)  106 us
    reduce_scatter x1, waiting for transfers between devices, body(): summed = lax.psum_scatter(moved, 'dp', scatter_dimension=2, tiled=True)  85 us
    all_to_all x1, blocking collectives, body(): lax.all_to_all(stacked, 'shard', split_axis=5, concat_axis=3, tiled=True)  59 us
    all_gather x1, waiting for transfers between devices, body(): stacked = lax.all_gather(fresh, 'dp', axis=2, tiled=True)  57.6 us
    unnamed x10, local copies, waits for them, and re-layouts  36.2 us
    all_to_all x2, local copies, waits for them, and re-layouts, body(): lax.all_to_all(stacked, 'shard', split_axis=5, concat_axis=3, tiled=True)  15.9 us
    all_gather x1, local copies, waits for them, and re-layouts, body(): stacked = lax.all_gather(fresh, 'dp', axis=2, tiled=True)  15.3 us
    all_to_all x2, local copies, waits for them, and re-layouts, body(): lax.all_to_all(pieces, 'shard', split_axis=3, concat_axis=5, tiled=True)  8.15 us
  transfers between devices with their start and end apart: 2, of which 2 were waited for; matrix products, arithmetic and copies ran while one was open for 0% of the time, Pallas kernels for 0%

commit v1 on v0

--- a/solution.py
+++ b/solution.py
@@ -27,7 +27,9 @@
     update = new_one / fix_one / (jnp.sqrt(new_two / fix_two) + 1e-08) + 0.1 * params
     new_params = params - learn * update
     fresh = new_params.astype(jnp.bfloat16).reshape(relations, 2, 1, 1, owned, width)
-    stacked = lax.all_gather(fresh, "dp", axis=2, tiled=True)
+    stacked = jnp.concatenate(
+        lax.all_to_all(jnp.stack(lax.axis_size("dp") * [fresh], 0), "dp", 0, 0), axis=2
+    )
     panel = lax.all_to_all(stacked, "shard", split_axis=5, concat_axis=3, tiled=True)
     panels = panel.reshape(relations, 2, width, panel_cols)
     return (new_params, new_one, new_two, panels)

time: 407 us -> 379 us (0.931)
  waiting for transfers between devices: 143 us -> 85.1 us
  blocking collectives: 165 us -> 196 us
    all_gather x1 -> x0, waiting for transfers between devices: 57.6 us -> none  [body(): stacked = lax.all_gather(fresh, 'dp', axis=2, tiled=True)]
    all_to_all x0 -> x1, blocking collectives: none -> 30.3 us  [body(): lax.all_to_all(jnp.stack(lax.axis_size('dp') * [fresh], 0), 'dp', 0, 0)]
    all_gather x1 -> x0, local copies, waits for them, and re-layouts: 15.3 us -> none  [body(): stacked = lax.all_gather(fresh, 'dp', axis=2, tiled=True)]
    reshape x0 -> x1, local copies, waits for them, and re-layouts: none -> 14 us  [body(): jnp.concatenate(lax.all_to_all(jnp.stack(lax.axis_size('dp') * [fresh], 0...]
  transfers between devices with their start and end apart: 2 -> 1, of which waited for: 2 -> 1; matrix products, arithmetic and copies ran while one was open for 0% -> 0% of each run, Pallas kernels for 0% -> 0%
where the time goes in v1:
time: 379 us; the launch traced here: 378 us
  blocking collectives  196 us (52%)
  waiting for transfers between devices  85.1 us (22%)
  local copies, waits for them, and re-layouts  77.4 us (20%)
  between operations  15.6 us (4%)
    all_to_all x1, blocking collectives, body(): lax.all_to_all(pieces, 'shard', split_axis=3, concat_axis=5, tiled=True)  106 us
    reduce_scatter x1, waiting for transfers between devices, body(): summed = lax.psum_scatter(moved, 'dp', scatter_dimension=2, tiled=True)  85.1 us
    all_to_all x1, blocking collectives, body(): lax.all_to_all(stacked, 'shard', split_axis=5, concat_axis=3, tiled=True)  59.8 us
    unnamed x10, local copies, waits for them, and re-layouts  36.2 us
    all_to_all x1, blocking collectives, body(): lax.all_to_all(jnp.stack(lax.axis_size('dp') * [fresh], 0), 'dp', 0, 0)  30.3 us
    all_to_all x2, local copies, waits for them, and re-layouts, body(): lax.all_to_all(stacked, 'shard', split_axis=5, concat_axis=3, tiled=True)  15.9 us
    reshape x1, local copies, waits for them, and re-layouts, body(): jnp.concatenate(lax.all_to_all(jnp.stack(lax.axis_size('dp') * [fresh], 0...  14 us
    all_to_all x2, local copies, waits for them, and re-layouts, body(): lax.all_to_all(pieces, 'shard', split_axis=3, concat_axis=5, tiled=True)  8.16 us
  transfers between devices with their start and end apart: 1, of which 1 were waited for; matrix products, arithmetic and copies ran while one was open for 0% of the time, Pallas kernels for 0%

profile of v1, /device:TPU:32, one launch (start us, length us, event | category | flops | bytes accessed | tf_op | source)
XLA Modules:
  0.0 377.7 jit_solution(16755498019997602773)
XLA Ops:
  7.2 0.0 reduce-scatter.2.cloned.1.call-start
  7.2 2.8 copy.31
  10.1 105.8 %all_to_all.38 = f32[1,2,8,32,16,128]{5,4,1,2,0,3:T(8,128)S(1)} all-to-all(f32[1,2,8,32,16,128]{5,4,1,2,0,3:T(8,128)S(1)} %copy.31), channel_id=1, replica_groups=mesh['dp'=8,'shard'=32] {'shard'}, dimensions={3} | all-to-all | bytes 8388608 | tf_op jit(solution)/shard_map/all_to_all | solution.py:15
  115.9 2.4 copy.32
  118.3 5.7 %copy.33 = f32[1,2,8,1,16,4096]{5,4,3,1,0,2:T(8,128)} copy(f32[1,2,8,1,16,4096]{5,3,4,2,1,0:T(1,128)S(1)} %bitcast.33) | data formatting | bytes 8388608 | tf_op jit(solution)/shard_map/all_to_all | solution.py:15
  124.0 0.0 copy-start.3
  124.0 0.0 copy-start
  124.0 0.0 copy-start.1
  124.0 0.0 copy-start.2
  124.1 0.0 reduce-scatter.2.cloned.1.call-update
  125.6 0.0 copy-done.3
  125.6 0.7 fusion
  126.2 85.1 %reduce-scatter.2.cloned.1.call-done = f32[1,2,1,1,16,4096]{5,4,3,1,0,2:T(8,128)} async-done(((f32[1,2,8,1,16,4096]{5,4,3,1,0,2:T(8,128)}), f32[1,2,1,1,16,4096]{5,4,3,1,0,2:T(8,128)}) %reduce-scatter.2.cloned.1.call-update) | async-done | bytes 524304 | tf_op jit(solution)/shard_map/reduce_scatter | solution.py:16
  211.3 0.0 copy-done
  211.3 0.0 copy-done.1
  211.3 0.0 copy-done.2
  211.3 3.1 convert_bitcast_fusion
  214.4 0.2 stack.3
  214.6 30.3 %all_to_all.39 = bf16[8,1,2,1,1,16,4096]{6,5,2,4,3,1,0:T(8,128)(2,1)S(1)} all-to-all(bf16[8,1,2,1,1,16,4096]{6,5,2,4,3,1,0:T(8,128)(2,1)S(1)} %stack.3), channel_id=1, replica_groups=mesh['dp'=8,'shard'=32] {'dp'}, dimensions={0} | all-to-all | bytes 4194304 | tf_op jit(solution)/shard_map/all_to_all | solution.py:31
  244.9 14.0 %copy.35 = bf16[1,2,8,1,16,4096]{4,2,1,3,0,5:T(8,128)(2,1)} copy(bf16[1,2,8,1,16,4096]{5,4,1,2,3,0:T(8,128)(2,1)S(1)} %bitcast.34) | data formatting | bytes 4194304 | tf_op jit(solution)/shard_map/reshape | solution.py:30
  258.9 19.7 %reshape.96 = bf16[32,2,16384]{2,1,0:T(2,128)(2,1)S(1)} reshape(bf16[4096,1,1,2,8,16]{5,4,3,2,1,0:T(8,128)(2,1)} %bitcast.31) | data formatting | bytes 4194304
  278.6 59.8 %all_to_all.40 = bf16[32,2,16384]{2,1,0:T(2,128)(2,1)} all-to-all(bf16[32,2,16384]{2,1,0:T(2,128)(2,1)S(1)} %reshape.96), channel_id=1, replica_groups=mesh['dp'=8,'shard'=32] {'shard'}, dimensions={0} | all-to-all | bytes 4194304 | tf_op jit(solution)/shard_map/all_to_all | solution.py:33
  338.5 16.5 %reshape.97 = bf16[4096,1,1,2,8,16]{5,4,3,2,1,0:T(8,128)(2,1)} reshape(bf16[32,2,16384]{2,1,0:T(2,128)(2,1)} %all_to_all.40) | data formatting | bytes 4194304
  355.0 13.7 %copy.38 = bf16[1,2,8,1,16,32,128]{6,5,4,2,1,3,0:T(8,128)(2,1)S(1)} copy(bf16[1,2,8,1,16,32,128]{4,2,1,6,5,3,0:T(8,128)(2,1)} %bitcast.32) | data formatting | bytes 4194304 | tf_op jit(solution)/shard_map/all_to_all | solution.py:33
  368.7 2.2 copy.37
Async XLA Ops:
  7.2 204.2 %reduce-scatter.2.cloned.1.call-start = ((), (), s32[]{:S(2)}) async-start(), calls=%async_computation.4 | async-start | bytes 4718592 | tf_op jit(solution)/shard_map/reduce_scatter | solution.py:16
  124.0 1.5 copy-start.3
  124.0 87.3 %copy-start = (f32[1,2,16,4096]{3,2,1,0:T(8,128)S(1)}, f32[1,2,16,4096]{3,2,1,0:T(8,128)}, u32[]{:S(2)}) copy-start(f32[1,2,16,4096]{3,2,1,0:T(8,128)} %param.8) | copy-start | bytes 1572868
  124.0 87.3 %copy-start.1 = (f32[1,2,16,4096]{3,2,1,0:T(8,128)S(1)}, f32[1,2,16,4096]{3,2,1,0:T(8,128)}, u32[]{:S(2)}) copy-start(f32[1,2,16,4096]{3,2,1,0:T(8,128)} %param.10) | copy-start | bytes 1572868
  124.0 87.3 %copy-start.2 = (f32[1,2,16,4096]{3,2,1,0:T(8,128)S(1)}, f32[1,2,16,4096]{3,2,1,0:T(8,128)}, u32[]{:S(2)}) copy-start(f32[1,2,16,4096]{3,2,1,0:T(8,128)} %param.9) | copy-start | bytes 1572868
Sparse Core Ops, SparseCore 0:
  124.2 87.0 reduce-scatter.1

commit v2 on v0

--- a/solution.py
+++ b/solution.py
@@ -28,7 +28,19 @@
     new_params = params - learn * update
     fresh = new_params.astype(jnp.bfloat16).reshape(relations, 2, 1, 1, owned, width)
     stacked = lax.all_gather(fresh, "dp", axis=2, tiled=True)
-    panel = lax.all_to_all(stacked, "shard", split_axis=5, concat_axis=3, tiled=True)
+
+    def lift_face_in(chunk, mesh_ax):
+        return jnp.concatenate(
+            lax.all_to_all(
+                jnp.stack(jnp.split(chunk, lax.axis_size(mesh_ax), axis=5), 0),
+                mesh_ax,
+                split_axis=0,
+                concat_axis=0,
+            ),
+            axis=3,
+        )
+
+    panel = lift_face_in(stacked, "shard")
     panels = panel.reshape(relations, 2, width, panel_cols)
     return (new_params, new_one, new_two, panels)
 

time: 407 us -> 355 us (0.87)
  local copies, waits for them, and re-layouts: 78.4 us -> 27.1 us
    unnamed x10 -> x41, local copies, waits for them, and re-layouts: 36.2 us -> 14.2 us
    all_gather x1 -> x0, local copies, waits for them, and re-layouts: 15.3 us -> none  [body(): stacked = lax.all_gather(fresh, 'dp', axis=2, tiled=True)]
    all_to_all x2 -> x1, local copies, waits for them, and re-layouts: 15.9 us -> 1.86 us  [lift_face_in(): lax.all_to_all(jnp.stack(jnp.split(chunk, lax.axis_size(mesh_ax), axis=5)...]
where the time goes in v2:
time: 355 us; the launch traced here: 354 us
  blocking collectives  165 us (46%)
  waiting for transfers between devices  143 us (40%)
  local copies, waits for them, and re-layouts  27.1 us (8%)
  between operations  15.6 us (4%)
  other arithmetic  3.88 us (1%)
    all_to_all x1, blocking collectives, body(): lax.all_to_all(pieces, 'shard', split_axis=3, concat_axis=5, tiled=True)  106 us
    reduce_scatter x1, waiting for transfers between devices, body(): summed = lax.psum_scatter(moved, 'dp', scatter_dimension=2, tiled=True)  85 us
    all_to_all x1, blocking collectives, lift_face_in(): lax.all_to_all(jnp.stack(jnp.split(chunk, lax.axis_size(mesh_ax), axis=5)...  58.9 us
    all_gather x1, waiting for transfers between devices, body(): stacked = lax.all_gather(fresh, 'dp', axis=2, tiled=True)  57.6 us
    unnamed x41, local copies, waits for them, and re-layouts  14.2 us
    all_to_all x2, local copies, waits for them, and re-layouts, body(): lax.all_to_all(pieces, 'shard', split_axis=3, concat_axis=5, tiled=True)  8.17 us
  transfers between devices with their start and end apart: 2, of which 2 were waited for; matrix products, arithmetic and copies ran while one was open for 0% of the time, Pallas kernels for 0%

profile of v2, /device:TPU:32, one launch (start us, length us, event | category | flops | bytes accessed | tf_op | source)
XLA Modules:
  0.0 354.1 jit_solution(9489471789073494876)
XLA Ops:
  7.2 0.0 reduce-scatter.2.cloned.1.call-start
  7.2 2.8 copy.54
  10.1 105.8 %all_to_all.23 = f32[1,2,8,32,16,128]{5,4,1,2,0,3:T(8,128)S(1)} all-to-all(f32[1,2,8,32,16,128]{5,4,1,2,0,3:T(8,128)S(1)} %copy.54), channel_id=1, replica_groups=mesh['dp'=8,'shard'=32] {'shard'}, dimensions={3} | all-to-all | bytes 8388608 | tf_op jit(solution)/shard_map/all_to_all | solution.py:15
  115.9 2.4 copy.55
  118.3 5.7 %copy.56 = f32[1,2,8,1,16,4096]{5,4,3,1,0,2:T(8,128)} copy(f32[1,2,8,1,16,4096]{5,3,4,2,1,0:T(1,128)S(1)} %bitcast.153) | data formatting | bytes 8388608 | tf_op jit(solution)/shard_map/all_to_all | solution.py:15
  124.1 0.0 copy-start.4
  124.1 0.0 copy-start.1
  124.1 0.0 copy-start.2
  124.1 0.0 copy-start.3
  124.1 0.0 reduce-scatter.2.cloned.1.call-update
  124.1 0.0 all-gather.3.cloned.1.call-start
  125.6 0.0 copy-done.4
  125.6 0.7 fusion
  126.3 85.0 %reduce-scatter.2.cloned.1.call-done = f32[1,2,1,1,16,4096]{5,4,3,1,0,2:T(8,128)} async-done(((f32[1,2,8,1,16,4096]{5,4,3,1,0,2:T(8,128)}), f32[1,2,1,1,16,4096]{5,4,3,1,0,2:T(8,128)}) %reduce-scatter.2.cloned.1.call-update) | async-done | bytes 524304 | tf_op jit(solution)/shard_map/reduce_scatter | solution.py:16
  211.3 0.0 copy-done.1
  211.3 0.0 copy-done.2
  211.4 0.0 copy-done.3
  211.4 3.2 fusion.1
  214.6 0.0 all-gather.3.cloned.1.call-update
  214.6 57.6 %all-gather.3.cloned.1.call-done = bf16[1,2,128,4096]{3,2,1,0:T(8,128)(2,1)} async-done(((bf16[1,2,16,4096]{3,2,1,0:T(8,128)(2,1)}), bf16[1,2,128,4096]{3,2,1,0:T(8,128)(2,1)}) %all-gather.3.cloned.1.call-update) | async-done | bytes 2097168 | tf_op jit(solution)/shard_map/all_gather | solution.py:30
  272.2 0.0 copy-start
  272.2 1.0 constant_dynamic-update-slice_fusion.31
  273.1 0.9 constant_dynamic-update-slice_fusion.30
  274.0 0.9 constant_dynamic-update-slice_fusion.29
  274.9 0.9 constant_dynamic-update-slice_fusion.28
  275.7 0.9 constant_dynamic-update-slice_fusion.27
  276.6 0.9 constant_dynamic-update-slice_fusion.26
  277.4 0.9 constant_dynamic-update-slice_fusion.25
  278.3 0.9 constant_dynamic-update-slice_fusion.24
  279.1 0.9 constant_dynamic-update-slice_fusion.23
  280.0 0.9 constant_dynamic-update-slice_fusion.22
  280.8 0.9 constant_dynamic-update-slice_fusion.21
  281.7 0.9 constant_dynamic-update-slice_fusion.20
  282.5 0.9 constant_dynamic-update-slice_fusion.19
  283.4 0.9 constant_dynamic-update-slice_fusion.18
  284.3 0.9 constant_dynamic-update-slice_fusion.17
  285.1 0.9 constant_dynamic-update-slice_fusion.16
  286.0 0.0 copy-done
  286.5 58.9 %all_to_all.24 = bf16[32,1,2,8,1,16,128]{6,5,3,2,4,1,0:T(8,128)(2,1)S(1)} all-to-all(bf16[32,1,2,8,1,16,128]{6,5,3,2,4,1,0:T(8,128)(2,1)S(1)} %constant_dynamic-update-slice_fusion), channel_id=1, replica_groups=mesh['dp'=8,'shard'=32] {'shard'}, dimensions={0} | all-to-all | bytes 4194304 | tf_op jit(solution)/shard_map/all_to_all | solution.py:34
  345.4 1.9 copy.58
  (16 shorter events, 0.5 us)
Async XLA Ops:
  7.2 204.2 %reduce-scatter.2.cloned.1.call-start = ((), (), s32[]{:S(2)}) async-start(), calls=%async_computation.3 | async-start | bytes 4718592 | tf_op jit(solution)/shard_map/reduce_scatter | solution.py:16
  124.1 1.6 copy-start.4
  124.1 87.3 %copy-start.1 = (f32[1,2,16,4096]{3,2,1,0:T(8,128)S(1)}, f32[1,2,16,4096]{3,2,1,0:T(8,128)}, u32[]{:S(2)}) copy-start(f32[1,2,16,4096]{3,2,1,0:T(8,128)} %param.8) | copy-start | bytes 1572868
  124.1 87.3 %copy-start.2 = (f32[1,2,16,4096]{3,2,1,0:T(8,128)S(1)}, f32[1,2,16,4096]{3,2,1,0:T(8,128)}, u32[]{:S(2)}) copy-start(f32[1,2,16,4096]{3,2,1,0:T(8,128)} %param.10) | copy-start | bytes 1572868
  124.1 87.3 %copy-start.3 = (f32[1,2,16,4096]{3,2,1,0:T(8,128)S(1)}, f32[1,2,16,4096]{3,2,1,0:T(8,128)}, u32[]{:S(2)}) copy-start(f32[1,2,16,4096]{3,2,1,0:T(8,128)} %param.9) | copy-start | bytes 1572868
  124.1 148.1 %all-gather.3.cloned.1.call-start = ((), (), s32[]{:S(2)}) async-start(), calls=%async_computation.4 | async-start | bytes 2359296 | tf_op jit(solution)/shard_map/all_gather | solution.py:30
  272.2 13.8 %copy-start = (bf16[1,2,128,4096]{3,2,1,0:T(8,128)(2,1)S(1)}, bf16[1,2,128,4096]{3,2,1,0:T(8,128)(2,1)}, u32[]{:S(2)}) copy-start(bf16[1,2,128,4096]{3,2,1,0:T(8,128)(2,1)} %all-gather.3.cloned.1.call-done) | copy-start | bytes 6291460
Sparse Core Ops, SparseCore 0:
  124.2 87.0 reduce-scatter.1
  214.7 57.4 all-gather.2
